TPU v7x, 512 devices: a whole 4x8x8 slice. The times are simulated.
512 devices in a mesh: req: 64 (over y, x, core), tp: 8 (over z).
Axes of the slice: x: 4, y: 8, z: 8, core: 2. Of those that a mesh axis runs over, the one named last changes fastest.
Arguments:
- hidden: bfloat16 [2048, 5, 2560], P('req', None, 'tp'), may hold values from -6 to 6
- norm_gain: bfloat16 [2560], replicated, may hold values from 0.099609375 to 1.8984375
- query_weight: bfloat16 [2560, 2560], P(None, 'tp'), may hold values from -0.125 to 0.125
- key_value_matrix: bfloat16 [2560, 8, 160], P(None, 'tp'), may hold values from -0.125 to 0.125
- output_weight: bfloat16 [2560, 2560], P('tp'), may hold values from -0.5 to 0.5
- key_value_cache: bfloat16 [2048, 64, 8, 160], P('req', None, 'tp'), as said below
- deal_order: int32 [2048], P('req'), may hold values from 0 to 2047, as said below
- cache_length: int32 [2048], P('req'), may hold values from 1 to 64, as said below
- accepted: int32 [2048], P('req'), may hold values from 1 to 5
Outputs:
- block_output: bfloat16 [2048, 5, 2560], P('req', None, 'tp')
- new_entries: bfloat16 [2048, 5, 8, 160], P('req', None, 'tp')
Inputs may be any that keep to these rules, and one draw needn't show every extreme that they name: deal_order is a permutation of the 2048 requests; slot i lies on index i // 32 of req, and request r arrives on index r // 32. Every index deals at most 1 of its requests to any one index, and exactly 1 to each of 32 indices. Cache entries of slot i at positions from cache_length[i] on are unused. `key_value_cache`: at positions below cache_length[i] the first 80 entries of each head are the keys, already rotated for their positions, and the last 80 the values.
All inputs are finite; a program needn't handle non-finite values.
Results may differ from a plain program's by a relative error of at most 0.0091.
Values may be sent and summed in bfloat16 or wider, within the bound.
No kernel may reach another device: no remote copies, remote signals or barrier semaphores. Data moves between devices by JAX's collectives and lax.ppermute only.
A program may use at most 128 MiB of HBM per device.

v0:
```python
import math
import jax
import jax.numpy as jnp
from jax import lax
from jax.sharding import PartitionSpec as P

HEAD_SIZE = 80
masked_score = -1e30


def rotate(values, positions):
    half_dim = HEAD_SIZE // 2
    frequency = 10000.0 ** (-2.0 * jnp.arange(half_dim, dtype=jnp.float32) / HEAD_SIZE)
    angles = positions.astype(jnp.float32)[..., None] * frequency
    cosine_part = jnp.cos(angles)
    sine_part = jnp.sin(angles)
    first_half = values[..., :half_dim]
    second_half = values[..., half_dim:]
    return jnp.concatenate(
        [
            first_half * cosine_part - second_half * sine_part,
            second_half * cosine_part + first_half * sine_part,
        ],
        axis=-1,
    )


def attend(query_rows, key_value_cache, fresh, cache_length):
    scale = 1.0 / math.sqrt(HEAD_SIZE)
    slot_count = query_rows.shape[0]
    verified = query_rows.shape[1]
    cache_keys = key_value_cache[..., :HEAD_SIZE]
    cache_values = key_value_cache[..., HEAD_SIZE:]
    fresh_keys = fresh[..., :HEAD_SIZE]
    fresh_values = fresh[..., HEAD_SIZE:]
    cache_scores = (
        jnp.einsum("rtghd,rcgd->rghtc", query_rows, cache_keys, preferred_element_type=jnp.float32)
        * scale
    )
    visible = jnp.arange(key_value_cache.shape[1], dtype=jnp.int32)[None, :] < cache_length[:, None]
    cache_scores = jnp.where(visible[:, None, None, None, :], cache_scores, masked_score)
    fresh_scores = (
        jnp.einsum("rtghd,rugd->rghtu", query_rows, fresh_keys, preferred_element_type=jnp.float32)
        * scale
    )
    causal = (
        jnp.arange(verified, dtype=jnp.int32)[:, None]
        >= jnp.arange(verified, dtype=jnp.int32)[None, :]
    )
    fresh_scores = jnp.where(causal[None, None, None, :, :], fresh_scores, masked_score)
    largest = jnp.maximum(jnp.max(cache_scores, axis=-1), jnp.max(fresh_scores, axis=-1))[..., None]
    cache_expos = jnp.exp(cache_scores - largest)
    fresh_expos = jnp.exp(fresh_scores - largest)
    totals = jnp.sum(cache_expos, axis=-1, keepdims=True) + jnp.sum(
        fresh_expos, axis=-1, keepdims=True
    )
    cache_weights = (cache_expos / totals).astype(jnp.bfloat16)
    fresh_weights = (fresh_expos / totals).astype(jnp.bfloat16)
    mixed = jnp.einsum(
        "rghtc,rcgd->rtghd", cache_weights, cache_values, preferred_element_type=jnp.float32
    )
    mixed = mixed + jnp.einsum(
        "rghtu,rugd->rtghd", fresh_weights, fresh_values, preferred_element_type=jnp.float32
    )
    return mixed.astype(jnp.bfloat16).reshape(slot_count, verified, -1)


def body(
    hidden,
    norm_gain,
    query_weight,
    key_value_matrix,
    output_weight,
    key_value_cache,
    deal_order,
    cache_length,
    accepted,
):
    slot_count = deal_order.shape[0]
    verified = hidden.shape[1]
    device_index = lax.axis_index("req")
    my_requests = device_index * slot_count + jnp.arange(slot_count, dtype=jnp.int32)
    piece = lax.all_gather(hidden, "req", axis=0, tiled=True)
    picker = (deal_order[:, None] == jnp.arange(piece.shape[0], dtype=jnp.int32)[None, :]).astype(
        jnp.bfloat16
    )
    dealt_rows = jnp.einsum(
        "in,ntf->itf", picker, piece, preferred_element_type=jnp.float32
    ).astype(jnp.bfloat16)
    features = lax.all_gather(dealt_rows, "tp", axis=2, tiled=True)
    widened = features.astype(jnp.float32)
    variance = jnp.mean(widened * widened, axis=-1, keepdims=True)
    normed = (widened * lax.rsqrt(variance + 1e-05) * norm_gain.astype(jnp.float32)).astype(
        jnp.bfloat16
    )
    heads_here = query_weight.shape[1] // HEAD_SIZE
    groups_here = key_value_matrix.shape[1]
    positions = cache_length[:, None] + jnp.arange(verified, dtype=jnp.int32)[None, :]
    query_rows = jnp.einsum("rtd,de->rte", normed, query_weight, preferred_element_type=jnp.float32)
    query_rows = query_rows.reshape(
        slot_count, verified, groups_here, heads_here // groups_here, HEAD_SIZE
    )
    query_rows = rotate(query_rows, positions[:, :, None, None]).astype(jnp.bfloat16)
    projected = jnp.einsum(
        "rtd,dge->rtge", normed, key_value_matrix, preferred_element_type=jnp.float32
    )
    fresh = jnp.concatenate(
        [rotate(projected[..., :HEAD_SIZE], positions[:, :, None]), projected[..., HEAD_SIZE:]],
        axis=-1,
    ).astype(jnp.bfloat16)
    keep = (jnp.arange(verified, dtype=jnp.int32)[None, :] < accepted[:, None])[:, :, None, None]
    new_entries = jnp.where(keep, fresh, jnp.zeros_like(fresh))
    mixed = attend(query_rows, key_value_cache, fresh, cache_length)
    partial_sum = jnp.einsum(
        "rte,ed->rtd", mixed, output_weight, preferred_element_type=jnp.float32
    )
    out_dealt = lax.psum_scatter(partial_sum, "tp", scatter_dimension=2, tiled=True).astype(
        jnp.bfloat16
    )
    piece_rows = lax.all_gather(out_dealt, "req", axis=0, tiled=True)
    piece_owners = lax.all_gather(deal_order, "req", axis=0, tiled=True)
    picker = (my_requests[:, None] == piece_owners[None, :]).astype(jnp.bfloat16)
    block_output = jnp.einsum(
        "jn,ntf->jtf", picker, piece_rows, preferred_element_type=jnp.float32
    ).astype(jnp.bfloat16)
    return (block_output, new_entries)


def solution(mesh):
    placed = (
        P("req", None, "tp"),
        P(),
        P(None, "tp"),
        P(None, "tp", None),
        P("tp", None),
        P("req", None, "tp", None),
        P("req"),
        P("req"),
        P("req"),
    )
    return jax.shard_map(
        body,
        mesh=mesh,
        in_specs=placed,
        out_specs=(P("req", None, "tp"), P("req", None, "tp", None)),
        check_vma=False,
    )
```

profile of v0, /device:TPU:1, one launch (start us, length us, event | category | flops | bytes accessed | tf_op | source)
XLA Modules:
  0.0 338.5 jit_solution(15841835390689357700)
XLA Ops:
  7.2 0.0 copy-start
  7.2 0.0 all-gather.3.cloned.1.call-start
  7.2 0.7 all-gather.3.cloned.1.call-update
  7.9 0.0 reduce-scatter.4.cloned.1.call-start
  8.0 0.7 convert_element_type.71
  8.7 0.7 add_convert_fusion
  9.3 0.1 copy.46
  9.4 0.7 iota_compare_fusion.1
  10.2 0.5 multiply_cosine_fusion
  10.7 93.9 %all-gather.3.cloned.1.call-done = bf16[2048,5,320]{2,0,1:T(8,128)(2,1)} async-done(((bf16[32,5,320]{2,0,1:T(8,128)(2,1)}), bf16[2048,5,320]{2,0,1:T(8,128)(2,1)}) %all-gather.3.cloned.1.call-update) | async-done | bytes 6553616 | tf_op jit(solution)/shard_map/all_gather | solution.py:83
  104.6 4.7 %convolution_convert_fusion.1 = bf16[32,5,320]{2,0,1:T(8,128)(2,1)S(1)} fusion(bf16[2048,5,320]{2,0,1:T(8,128)(2,1)} %all-gather.3.cloned.1.call-done, s32[32]{0:T(128)} %param.15), kind=kOutput, calls=%fused_computation.21 | convolution fusion | flops 209831936 | bytes 6656128 | tf_op jit(solution)/shard_map/in,ntf->itf/dot_general | solution.py:87
  109.3 0.4 copy.43
  109.7 55.1 %all_gather.14 = bf16[32,5,2560]{0,1,2:T(8,128)(2,1)} all-gather(bf16[32,5,320]{0,1,2:T(8,128)(2,1)S(1)} %copy.43), channel_id=1, replica_groups=mesh['req'=64,'tp'=8] {'tp'}, dimensions={2}, use_global_device_ids=true | all-gather | bytes 921600 | tf_op jit(solution)/shard_map/all_gather | solution.py:90
  164.9 4.4 %copy.44 = bf16[32,5,2560]{2,0,1:T(8,128)(2,1)S(1)} copy(bf16[32,5,2560]{0,1,2:T(8,128)(2,1)} %all_gather.14) | data formatting | bytes 1638400 | tf_op jit(solution)/shard_map/all_gather | solution.py:90
  169.3 0.2 fusion
  169.5 1.7 convolution_bitcast_fusion.1
  171.2 0.1 slice_bitcast_fusion.4
  171.3 0.6 copy-done.1
  171.9 0.4 fusion.41
  172.3 0.8 fusion.5
  173.1 0.2 reshape.324
  173.3 0.2 fusion.49
  173.5 0.1 maximum_bitcast_fusion
  173.6 0.5 fusion.24
  174.1 1.4 fusion.51
  175.5 0.6 fusion.50
  176.1 0.3 fusion.22
  176.3 0.4 fusion.21
  176.8 0.8 convolution_bitcast_fusion
  177.6 0.4 fusion.13
  178.0 0.1 copy.53
  178.1 0.1 reshape.332
  178.2 0.6 fusion.3
  178.8 5.5 %copy.64 = f32[32,5,2560]{0,1,2:T(8,128)} copy(f32[32,5,2560]{2,0,1:T(8,128)S(1)} %fusion.3) | data formatting | bytes 3276800
  184.3 8.0 %reshape.347 = f32[2560,160]{1,0:T(8,128)} reshape(f32[2560,5,32]{2,1,0:T(8,128)} %bitcast.87) | data formatting | bytes 3276800
  192.4 0.0 reduce-scatter.4.cloned.1.call-update
  192.4 0.0 all-gather.5.cloned.1.call-start
  192.4 39.6 %reduce-scatter.4.cloned.1.call-done = f32[320,160]{1,0:T(8,128)} async-done(((f32[2560,160]{1,0:T(8,128)}), f32[320,160]{1,0:T(8,128)}) %reduce-scatter.4.cloned.1.call-update) | async-done | bytes 204816
  232.1 1.2 reshape.348
  233.3 1.0 copy.65
  234.3 0.0 all-gather.5.cloned.1.call-update
  234.3 1.3 dynamic-slice
  236.3 0.3 dynamic-update-slice
  236.5 21.3 %all-reduce = s32[2048]{0:T(1024)S(1)} all-reduce(s32[2048]{0:T(1024)S(1)} %dynamic-update-slice), channel_id=1, replica_groups=mesh['req'=64,'tp'=8] {'req'}, use_global_device_ids=true, to_apply=%add | all-reduce | flops 2048 | bytes 16384
  257.9 1.0 slice.51
  258.9 0.8 fusion.44
  259.7 67.0 %all-gather.5.cloned.1.call-done = bf16[2048,5,320]{2,0,1:T(8,128)(2,1)} async-done(((bf16[32,5,320]{2,0,1:T(8,128)(2,1)}), bf16[2048,5,320]{2,0,1:T(8,128)(2,1)}) %all-gather.5.cloned.1.call-update) | async-done | bytes 6553616 | tf_op jit(solution)/shard_map/all_gather | solution.py:120
  326.7 5.3 %convolution_convert_fusion = bf16[32,5,320]{2,0,1:T(8,128)(2,1)} fusion(bf16[2048,5,320]{2,0,1:T(8,128)(2,1)} %all-gather.5.cloned.1.call-done, s32[2048]{0:T(1024)S(1)} %all-reduce, s32[32]{0:T(128)S(1)} %iota_add_fusion), kind=kOutput, calls=%fused_computation.20 | convolution fusion | flops 209831936 | bytes 6664320 | tf_op jit(solution)/shard_map/jn,ntf->jtf/dot_general | solution.py:123
  (18 shorter events, 0.1 us)
Async XLA Ops:
  7.2 171.1 %copy-start = (bf16[320,2560]{1,0:T(8,128)(2,1)S(1)}, bf16[320,2560]{1,0:T(8,128)(2,1)}, u32[]{:S(2)}) copy-start(bf16[320,2560]{1,0:T(8,128)(2,1)} %param.13) | copy-start | bytes 4915204
  7.2 97.5 %all-gather.3.cloned.1.call-start = ((), (), s32[]{:S(2)}) async-start(), calls=%async_computation.1 | async-start | bytes 7987200 | tf_op jit(solution)/shard_map/all_gather | solution.py:83
  7.9 224.2 %reduce-scatter.4.cloned.1.call-start = ((), (), s32[]{:S(2)}) async-start(), calls=%async_computation.3 | async-start | bytes 2949120
  169.2 3.0 copy-start.4
  171.2 0.7 copy-start.1
  173.5 1.9 copy-start.2
  192.4 43.9 %copy-start.3 = (s32[32]{0:T(128)S(1)}, s32[32]{0:T(128)}, u32[]{:S(2)}) copy-start(s32[32]{0:T(128)} %param.15) | copy-start | bytes 388
  192.4 65.5 %copy-start.5 = (s32[32]{0:T(128)S(1)}, s32[32]{0:T(128)}, u32[]{:S(2)}) copy-start(s32[32]{0:T(128)} %param.17) | copy-start | bytes 388
  192.4 134.3 %all-gather.5.cloned.1.call-start = ((), (), s32[]{:S(2)}) async-start(), calls=%async_computation.2 | async-start | bytes 7987200 | tf_op jit(solution)/shard_map/all_gather | solution.py:120
Sparse Core Ops, SparseCore 0:
  11.3 93.2 all-gather.2
  192.5 39.5 reduce-scatter.3
  235.9 90.6 all-gather.4
where the time goes:
time: 339 us; the launch traced here: 338 us
  waiting for transfers between devices  201 us (59%)
  blocking collectives  76.4 us (23%)
  local copies, waits for them, and re-layouts  24.5 us (7%)
  matrix products  16.2 us (5%)
  between operations  14.6 us (4%)
  other arithmetic  5.35 us (2%)
    all_gather x1, waiting for transfers between devices, body(): piece = lax.all_gather(hidden, 'req', axis=0, tiled=True)  93.9 us
    all_gather x1, waiting for transfers between devices, body(): piece_rows = lax.all_gather(out_dealt, 'req', axis=0, tiled=True)  67 us
    all_gather x1, blocking collectives, body(): features = lax.all_gather(dealt_rows, 'tp', axis=2, tiled=True)  55.1 us
    unnamed x4, waiting for transfers between devices  40.3 us
    unnamed x1, blocking collectives  21.3 us
    unnamed x19, local copies, waits for them, and re-layouts  17.9 us
  transfers between devices with their start and end apart: 3, of which 3 were waited for; matrix products, arithmetic and copies ran while one was open for 2% of the time, Pallas kernels for 0%

commit v1 on v0

--- a/solution.py
+++ b/solution.py
@@ -80,7 +80,8 @@
     verified = hidden.shape[1]
     device_index = lax.axis_index("req")
     my_requests = device_index * slot_count + jnp.arange(slot_count, dtype=jnp.int32)
-    piece = lax.all_gather(hidden, "req", axis=0, tiled=True)
+    sent = jnp.stack([hidden] * lax.axis_size("req"))
+    piece = jnp.concatenate(lax.all_to_all(sent, "req", 0, 0), axis=0)
     picker = (deal_order[:, None] == jnp.arange(piece.shape[0], dtype=jnp.int32)[None, :]).astype(
         jnp.bfloat16
     )

time: 339 us -> 437 us (1.29)
  waiting for transfers between devices: 201 us -> 279 us
  starting transfers between devices: 0.12 us -> 12.2 us
  local copies, waits for them, and re-layouts: 24.5 us -> 32.9 us
    all_to_all x0 -> x1, waiting for transfers between devices: none -> 169 us  [body(): piece = jnp.concatenate(lax.all_to_all(sent, 'req', 0, 0), axis=0)]
    all_gather x1 -> x0, waiting for transfers between devices: 93.9 us -> none  [body(): piece = lax.all_gather(hidden, 'req', axis=0, tiled=True)]
    all_to_all x0 -> x1, starting transfers between devices: none -> 12.1 us  [body(): piece = jnp.concatenate(lax.all_to_all(sent, 'req', 0, 0), axis=0)]
    another operation x1 -> x2, local copies, waits for them, and re-layouts: 0.08 us -> 4.94 us  [the longest x1 4.86 us: body(): sent = jnp.stack([hidden] * lax.axis_size('req'))]
    unnamed x4 -> x3, waiting for transfers between devices: 40.3 us -> 42.9 us
    unnamed x19 -> x27, local copies, waits for them, and re-layouts: 17.9 us -> 17.3 us
  transfers between devices with their start and end apart: 3 -> 3, of which waited for: 3 -> 3; matrix products, arithmetic and copies ran while one was open for 2% -> 1% of each run, Pallas kernels for 0% -> 0%
where the time goes in v1:
time: 437 us
  waiting for transfers between devices  279 us (64%)
  blocking collectives  78.8 us (18%)
  local copies, waits for them, and re-layouts  32.9 us (8%)
  between operations  15 us (3%)
  matrix products  13.6 us (3%)
  starting transfers between devices  12.2 us (3%)
  other arithmetic  4.53 us (1%)
    all_to_all x1, waiting for transfers between devices, body(): piece = jnp.concatenate(lax.all_to_all(sent, 'req', 0, 0), axis=0)  169 us
    all_gather x1, waiting for transfers between devices, body(): piece_rows = lax.all_gather(out_dealt, 'req', axis=0, tiled=True)  67.2 us
    all_gather x1, blocking collectives, body(): features = lax.all_gather(dealt_rows, 'tp', axis=2, tiled=True)  57.8 us
    unnamed x3, waiting for transfers between devices  42.9 us
    unnamed x1, blocking collectives  21 us
    unnamed x27, local copies, waits for them, and re-layouts  17.3 us
    all_to_all x1, starting transfers between devices, body(): piece = jnp.concatenate(lax.all_to_all(sent, 'req', 0, 0), axis=0)  12.1 us
  transfers between devices with their start and end apart: 3, of which 3 were waited for; matrix products, arithmetic and copies ran while one was open for 1% of the time, Pallas kernels for 0%

profile of v1, /device:TPU:1, one launch (start us, length us, event | category | flops | bytes accessed | tf_op | source)
XLA Modules:
  0.0 436.5 jit_solution(15037796194475624628)
XLA Ops:
  7.2 0.0 copy-start
  7.2 4.9 %stack.2 = bf16[64,32,5,320]{3,1,2,0:T(8,128)(2,1)} broadcast(bf16[32,5,320]{2,0,1:T(8,128)(2,1)} %param.9), dimensions={1,2,3} | broadcast | bytes 6656000 | tf_op jit(solution)/shard_map/stack | solution.py:83
  12.0 12.1 %all-to-all-start = ((bf16[64,32,5,320]{3,1,2,0:T(8,128)(2,1)}), bf16[64,32,5,320]{3,1,2,0:T(8,128)(2,1)}, u32[]{:S(2)}, u32[]{:S(2)}) async-start(bf16[64,32,5,320]{3,1,2,0:T(8,128)(2,1)} %stack.2), calls=%async_computation | async-start | bytes 15728640 | tf_op jit(solution)/shard_map/all_to_all | solution.py:84
  24.1 0.0 reduce-scatter.4.cloned.1.call-start
  24.2 0.6 convert_element_type.71
  24.8 0.1 copy.52
  24.9 0.6 iota_compare_fusion.3
  25.5 0.1 iota_compare_fusion.1
  25.6 0.5 multiply_cosine_fusion
  26.1 169.3 %all-to-all-done = bf16[64,32,5,320]{3,1,2,0:T(8,128)(2,1)} async-done(((bf16[64,32,5,320]{3,1,2,0:T(8,128)(2,1)}), bf16[64,32,5,320]{3,1,2,0:T(8,128)(2,1)}, u32[]{:S(2)}, u32[]{:S(2)}) %all-to-all-start) | async-done | bytes 6553632 | tf_op jit(solution)/shard_map/all_to_all | solution.py:84
  195.4 4.2 copy.47
  199.6 2.1 convolution_convert_fusion.1
  201.7 0.4 copy.49
  202.1 57.8 %all_gather.10 = bf16[32,5,2560]{0,1,2:T(8,128)(2,1)} all-gather(bf16[32,5,320]{0,1,2:T(8,128)(2,1)S(1)} %copy.49), channel_id=1, replica_groups=mesh['req'=64,'tp'=8] {'tp'}, dimensions={2}, use_global_device_ids=true | all-gather | bytes 921600 | tf_op jit(solution)/shard_map/all_gather | solution.py:91
  259.9 4.4 %copy.50 = bf16[32,5,2560]{2,0,1:T(8,128)(2,1)S(1)} copy(bf16[32,5,2560]{0,1,2:T(8,128)(2,1)} %all_gather.10) | data formatting | bytes 1638400 | tf_op jit(solution)/shard_map/all_gather | solution.py:91
  264.3 0.2 fusion
  264.6 1.7 convolution_bitcast_fusion.1
  266.3 0.4 fusion.41
  266.7 0.1 slice_bitcast_fusion.4
  266.8 0.8 fusion.5
  267.6 0.2 reshape.330
  267.8 0.2 fusion.49
  268.1 0.1 maximum_bitcast_fusion
  268.2 0.5 fusion.24
  268.7 1.4 fusion.51
  270.0 0.6 fusion.50
  270.6 0.3 fusion.22
  270.9 0.4 fusion.21
  271.4 0.8 convolution_bitcast_fusion
  272.2 0.4 fusion.13
  272.6 0.1 copy.59
  272.7 0.1 reshape.338
  272.8 0.6 fusion.3
  273.4 5.5 %copy.71 = f32[32,5,2560]{0,1,2:T(8,128)} copy(f32[32,5,2560]{2,0,1:T(8,128)S(1)} %fusion.3) | data formatting | bytes 3276800
  278.9 8.0 %reshape.353 = f32[2560,160]{1,0:T(8,128)} reshape(f32[2560,5,32]{2,1,0:T(8,128)} %bitcast.88) | data formatting | bytes 3276800
  286.9 0.0 reduce-scatter.4.cloned.1.call-update
  286.9 0.0 all-gather.2.cloned.1.call-start
  287.0 42.9 %reduce-scatter.4.cloned.1.call-done = f32[320,160]{1,0:T(8,128)} async-done(((f32[2560,160]{1,0:T(8,128)}), f32[320,160]{1,0:T(8,128)}) %reduce-scatter.4.cloned.1.call-update) | async-done | bytes 204816
  329.8 1.2 reshape.354
  331.1 1.0 copy.72
  332.0 0.0 all-gather.2.cloned.1.call-update
  332.1 1.3 dynamic-slice
  334.0 0.3 dynamic-update-slice
  334.3 21.0 %all-reduce = s32[2048]{0:T(1024)S(1)} all-reduce(s32[2048]{0:T(1024)S(1)} %dynamic-update-slice), channel_id=1, replica_groups=mesh['req'=64,'tp'=8] {'req'}, use_global_device_ids=true, to_apply=%add | all-reduce | flops 2048 | bytes 16384
  355.3 1.0 slice.51
  356.3 0.8 fusion.44
  357.1 67.2 %all-gather.2.cloned.1.call-done = bf16[2048,5,320]{2,0,1:T(8,128)(2,1)} async-done(((bf16[32,5,320]{2,0,1:T(8,128)(2,1)}), bf16[2048,5,320]{2,0,1:T(8,128)(2,1)}) %all-gather.2.cloned.1.call-update) | async-done | bytes 6553616 | tf_op jit(solution)/shard_map/all_gather | solution.py:121
  424.4 5.3 %convolution_convert_fusion = bf16[32,5,320]{2,0,1:T(8,128)(2,1)} fusion(bf16[2048,5,320]{2,0,1:T(8,128)(2,1)} %all-gather.2.cloned.1.call-done, s32[2048]{0:T(1024)S(1)} %all-reduce, s32[32]{0:T(128)S(1)} %iota_add_fusion), kind=kOutput, calls=%fused_computation.20 | convolution fusion | flops 209831936 | bytes 6664320 | tf_op jit(solution)/shard_map/jn,ntf->jtf/dot_general | solution.py:124
  (27 shorter events, 0.1 us)
Async XLA Ops:
  7.2 265.6 %copy-start = (bf16[320,2560]{1,0:T(8,128)(2,1)S(1)}, bf16[320,2560]{1,0:T(8,128)(2,1)}, u32[]{:S(2)}) copy-start(bf16[320,2560]{1,0:T(8,128)(2,1)} %param.13) | copy-start | bytes 4915204
  12.0 12.2 %copy-start.4 = (bf16[2560]{0:T(1024)(128)(2,1)S(1)}, bf16[2560]{0:T(1024)(128)(2,1)}, u32[]{:S(2)}) copy-start(bf16[2560]{0:T(1024)(128)(2,1)} %param.10) | copy-start | bytes 15364
  12.0 12.8 %copy-start.5 = (s32[32]{0:T(128)S(1)}, s32[32]{0:T(128)}, u32[]{:S(2)}) copy-start(s32[32]{0:T(128)} %param.16) | copy-start | bytes 388
  12.0 183.4 %all-to-all-start = ((bf16[64,32,5,320]{3,1,2,0:T(8,128)(2,1)}), bf16[64,32,5,320]{3,1,2,0:T(8,128)(2,1)}, u32[]{:S(2)}, u32[]{:S(2)}) async-start(bf16[64,32,5,320]{3,1,2,0:T(8,128)(2,1)} %stack.2), calls=%async_computation | async-start | bytes 15728640 | tf_op jit(solution)/shard_map/all_to_all | solution.py:84
  24.1 305.7 %reduce-scatter.4.cloned.1.call-start = ((), (), s32[]{:S(2)}) async-start(), calls=%async_computation.3 | async-start | bytes 2949120
  259.9 4.6 %copy-start.3 = (f32[2560]{0:T(1024)S(1)}, f32[2560]{0:T(1024)}, u32[]{:S(2)}) copy-start(f32[2560]{0:T(1024)} %convert_element_type.71) | copy-start | bytes 30724
  264.3 2.5 copy-start.8
  266.3 1.3 copy-start.1
  267.6 1.1 copy-start.6
  268.1 2.0 copy-start.2
  286.9 47.1 %copy-start.7 = (s32[32]{0:T(128)S(1)}, s32[32]{0:T(128)}, u32[]{:S(2)}) copy-start(s32[32]{0:T(128)} %param.15) | copy-start | bytes 388
  286.9 68.4 %copy-start.9 = (s32[32]{0:T(128)S(1)}, s32[32]{0:T(128)}, u32[]{:S(2)}) copy-start(s32[32]{0:T(128)} %param.17) | copy-start | bytes 388
  286.9 137.4 %all-gather.2.cloned.1.call-start = ((), (), s32[]{:S(2)}) async-start(), calls=%async_computation.2 | async-start | bytes 7987200 | tf_op jit(solution)/shard_map/all_gather | solution.py:121
Sparse Core Ops, SparseCore 0:
  287.0 42.7 reduce-scatter.3
  333.7 90.6 all-gather.1
